TPU v7x, 512 devices: a whole 4x4x16 slice. The times are simulated.
512 devices in a mesh: ctx: 64 (over z, x_hi, core), head: 8 (over y, x_lo).
Axes of the slice: x: 4 (x_hi: 2, x_lo: 2; x = x_hi * 2 + x_lo), y: 4, z: 16, core: 2. Of those that a mesh axis runs over, the one named last changes fastest.
Arguments:
- tokens: bfloat16 [8192, 4096], P('ctx'), may hold values from -6 to 6
- norm_gain: float32 [4096], replicated, may hold values from 0.25 to 1.75
- w_query: bfloat16 [4096, 4096], P('ctx', 'head'), may hold values from -0.09375 to 0.09375
- w_key: bfloat16 [4096, 1024], P('ctx', 'head'), may hold values from -0.09375 to 0.09375
- w_value: bfloat16 [4096, 1024], P('ctx', 'head'), may hold values from -0.09375 to 0.09375
- w_out: bfloat16 [4096, 4096], P('head', 'ctx'), may hold values from -0.09375 to 0.09375
- row_map: int32 [8192], P('ctx'), may hold values from 0 to 8191, as said below
- doc_lengths: int32 [32], replicated, may hold values from 1 to 2048, 8192 in all
- doc_labels: int32 [32], replicated, may hold values from 0 to 1, as said below
Outputs:
- residual_out: bfloat16 [8192, 4096], P('ctx', 'head')
- refusal_direction: float32 [4096], P('head')
Inputs may be any that keep to these rules, and one draw needn't show every extreme that they name: `row_map`: the rows of ctx index c are two runs of 64 consecutive positions, run b(c) and run 2 * 64 - 1 - b(c) of the pack, b a permutation drawn from the seed; every position appears once. `doc_labels`: at least one prompt of each class.
All inputs are finite; a program needn't handle non-finite values.
Results may differ from a plain program's by a relative error of at most 0.008.
Values may be sent and summed in bfloat16 or wider, within the bound.
No kernel may reach another device: no remote copies, remote signals or barrier semaphores. Data moves between devices by JAX's collectives and lax.ppermute only.
A program may use at most 64 MiB of HBM per device.

v0:
```python
import math
import jax
import jax.numpy as jnp
from jax import lax
from jax.sharding import Mesh
from jax.sharding import PartitionSpec as P

HEADS = 32
KV_HEADS = 8
HEAD_DIM = 128
MOST = 2048
RUN = 64
ROPE_BASE = 500000.0
NEG_FILL = -1e30
CTX = ("z", "xh", "c")
HEAD = ("y", "xl")


def doc_layout(row_map, doc_lengths):
    doc_ends = jnp.cumsum(doc_lengths)
    doc_starts = doc_ends - doc_lengths
    doc_index = jnp.sum((row_map[:, None] >= doc_ends[None, :]).astype(jnp.int32), 1)
    member = doc_index[:, None] == jnp.arange(doc_ends.shape[0], dtype=jnp.int32)[None, :]
    in_doc = row_map - jnp.sum(jnp.where(member, doc_starts[None, :], 0), 1)
    return (doc_index, in_doc, doc_ends)


def rotate(values, in_doc):
    head_dim = values.shape[-1]
    half_dim = head_dim // 2
    inv_freq = jnp.exp(
        jnp.arange(half_dim).astype(jnp.float32) * (-2.0 * math.log(ROPE_BASE) / head_dim)
    )
    angles = in_doc.astype(jnp.float32)[:, None] * inv_freq[None, :]
    shape_out = (angles.shape[0],) + (1,) * (values.ndim - 2) + (half_dim,)
    cosine = jnp.cos(angles).reshape(shape_out)
    sine_val = jnp.sin(angles).reshape(shape_out)
    front_half = values[..., :half_dim]
    back_half = values[..., half_dim:]
    return jnp.concatenate(
        [front_half * cosine - back_half * sine_val, back_half * cosine + front_half * sine_val], -1
    )


def rms_norm(tokens, norm_gain):
    wide_tokens = tokens.astype(jnp.float32)
    row_scale = lax.rsqrt(jnp.mean(wide_tokens * wide_tokens, -1, keepdims=True) + 1e-05)
    return (wide_tokens * row_scale * norm_gain).astype(jnp.bfloat16)


def swap_cat(x, axis_name):
    return jnp.concatenate([x, lax.ppermute(x, axis_name, [(0, 1), (1, 0)])], 0)


def gather_z(x):
    return lax.all_gather(x, "z", axis=0, tiled=True)


def gather_pair(x):
    return swap_cat(swap_cat(x, "xh"), "c")


def relative_index():
    return (
        lax.axis_index("c") ^ jnp.arange(2, dtype=jnp.int32),
        lax.axis_index("xh") ^ jnp.arange(2, dtype=jnp.int32),
    )


def to_gathered_order(x, sizes):
    nz, nxh, nc = sizes
    c_idx, xh_idx = relative_index()
    y = jnp.transpose(x.reshape(x.shape[0], nz, nxh, nc, x.shape[-1]), (0, 3, 2, 1, 4))
    y = jnp.take(jnp.take(y, c_idx, axis=1), xh_idx, axis=2)
    return y.reshape(x.shape)


def from_gathered_order(x, sizes):
    nz, nxh, nc = sizes
    c_idx, xh_idx = relative_index()
    y = x.reshape(x.shape[0], nc, nxh, nz, x.shape[-1])
    y = jnp.take(jnp.take(y, c_idx, axis=1), xh_idx, axis=2)
    return jnp.transpose(y, (0, 3, 2, 1, 4)).reshape(x.shape)


def reduce_scatter_head(x, head_sizes):
    ny, nxl = head_sizes
    rows, width = x.shape
    xl = lax.axis_index("xl")
    y = lax.axis_index("y")
    grouped = x.reshape(rows, ny, nxl, width // (ny * nxl))
    kept = jnp.take(grouped, xl, axis=2)
    sent = jnp.take(grouped, (xl + 1) % nxl, axis=2).astype(jnp.bfloat16)
    summed = kept + lax.ppermute(sent, "xl", [(0, 1), (1, 0)]).astype(jnp.float32)
    acc = jnp.take(summed, y, axis=1)
    for shift in range(1, ny):
        piece = jnp.take(summed, (y + shift) % ny, axis=1).astype(jnp.bfloat16)
        acc = acc + lax.ppermute(piece, "y", [(i, (i + shift) % ny) for i in range(ny)]).astype(
            jnp.float32
        )
    return acc


def make_local(sizes, head_sizes):
    nz, nxh, nc = sizes
    nctx = nz * nxh * nc

    def local(tokens, norm_gain, w_query, w_key, w_value, w_out, row_map, doc_lengths, doc_labels):
        tok_rows, width = tokens.shape
        d_rows = w_query.shape[0]
        q_cols = w_query.shape[1]
        kv_cols = w_key.shape[1]
        group_size = q_cols // kv_cols
        runs_here = tok_rows // RUN
        total_runs = runs_here * nctx
        win_runs = MOST // RUN + 1
        normed = rms_norm(tokens, norm_gain)
        doc_index, in_doc, doc_ends = doc_layout(row_map, doc_lengths)
        qkv_cols = q_cols + 2 * kv_cols
        out_cols = w_out.shape[0]
        w_z = gather_z(jnp.concatenate([w_query, w_key, w_value, w_out.T], axis=1))
        w_o = gather_pair(w_z[:, qkv_cols:]).reshape(nctx, d_rows, out_cols)
        w_proj = w_z[:, :qkv_cols]
        pair = ("xh", "c")
        npair = nxh * nc
        me = lax.axis_index("xh") * nc + lax.axis_index("c")
        quarters = jnp.transpose(
            normed.reshape(tok_rows, nz, nxh, nc, d_rows), (0, 2, 3, 1, 4)
        ).reshape(tok_rows, npair, nz * d_rows)
        perms = [[(i, i ^ flip) for i in range(npair)] for flip in range(1, npair)]
        theirs = [
            lax.ppermute(jnp.take(quarters, me ^ flip, axis=1), pair, perm)
            for flip, perm in zip(range(1, npair), perms)
        ]
        stacked = jnp.concatenate([jnp.take(quarters, me, axis=1)] + theirs, axis=0)
        parts = jnp.dot(stacked, w_proj, preferred_element_type=jnp.float32)
        rows = tok_rows
        on_chip = lax.ppermute(
            jnp.concatenate([parts[rows : 2 * rows], parts[3 * rows : 4 * rows]]), pair, perms[0]
        )
        across = lax.ppermute(parts[2 * rows : 3 * rows] + on_chip[rows:], pair, perms[1])
        proj = parts[:rows] + on_chip[:rows] + across
        queries = proj[:, :q_cols].reshape(tok_rows, group_size, HEAD_DIM)
        key_proj = proj[:, q_cols : q_cols + kv_cols]
        value_proj = proj[:, q_cols + kv_cols :].astype(jnp.bfloat16)
        queries = rotate(queries, in_doc).astype(jnp.bfloat16)
        key_proj = rotate(key_proj, in_doc).astype(jnp.bfloat16)
        assert 2 * tok_rows == 2 * kv_cols
        pos_row = jnp.concatenate([row_map // RUN, row_map % RUN]).astype(jnp.bfloat16)[None, :]
        kv_buf = jnp.concatenate(
            [jnp.concatenate([key_proj, value_proj], axis=1), jnp.pad(pos_row, ((0, 7), (0, 0)))],
            axis=0,
        )
        kv = gather_pair(gather_z(kv_buf)).reshape(nctx, tok_rows + 8, 2 * kv_cols)
        pos_code = kv[:, tok_rows, :].astype(jnp.int32)
        key_pos_all = pos_code[:, :tok_rows] * RUN + pos_code[:, tok_rows:]
        kv_halves = kv[:, :tok_rows].reshape(total_runs, RUN, 2 * kv_cols)
        pos_halves = key_pos_all.reshape(total_runs, RUN)
        run_of_half = pos_halves[:, 0] // RUN
        half_of_run = (
            jnp.zeros((total_runs,), jnp.int32)
            .at[run_of_half]
            .set(jnp.arange(total_runs, dtype=jnp.int32))
        )
        q_pos = row_map.reshape(runs_here, RUN)
        q_start = (row_map - in_doc).reshape(runs_here, RUN)
        q_run = q_pos[:, 0] // RUN
        first_run = jnp.maximum(q_run - (win_runs - 1), 0)
        win = first_run[:, None] + jnp.arange(win_runs, dtype=jnp.int32)[None, :]
        win_halves = half_of_run[win]
        kv_win = kv_halves[win_halves].reshape(runs_here, win_runs * RUN, 2 * kv_cols)
        k_pos = pos_halves[win_halves].reshape(runs_here, win_runs * RUN)
        k_win = kv_win[..., :kv_cols]
        v_win = kv_win[..., kv_cols:]
        q_runs = queries.reshape(runs_here, RUN, group_size, HEAD_DIM)
        scale_factor = HEAD_DIM ** (-0.5)
        scores = (
            jnp.einsum("rqgd,rkd->rgqk", q_runs, k_win, preferred_element_type=jnp.float32)
            * scale_factor
        )
        allowed = (k_pos[:, None, :] >= q_start[:, :, None]) & (
            k_pos[:, None, :] <= q_pos[:, :, None]
        )
        allowed = allowed[:, None]
        scores = jnp.where(allowed, scores, NEG_FILL)
        row_top = jnp.max(scores, -1, keepdims=True)
        weights = jnp.where(allowed, jnp.exp(scores - row_top), 0.0)
        row_sum = jnp.sum(weights, -1, keepdims=True)
        mixed = (
            jnp.einsum(
                "rgqk,rkd->rgqd",
                weights.astype(jnp.bfloat16),
                v_win,
                preferred_element_type=jnp.float32,
            )
            / row_sum
        ).astype(jnp.bfloat16)
        attended = jnp.transpose(mixed, (0, 2, 1, 3)).reshape(tok_rows, q_cols)
        partial_g = jnp.einsum("tk,jdk->tjd", attended, w_o, preferred_element_type=jnp.float32)
        partial_out = from_gathered_order(partial_g, sizes).reshape(tok_rows, width)
        head_share = reduce_scatter_head(partial_out, head_sizes)
        col_width = head_share.shape[1]
        head_idx = lax.axis_index("y") * head_sizes[1] + lax.axis_index("xl")
        own_cols = lax.dynamic_slice_in_dim(tokens, head_idx * col_width, col_width, 1)
        residual_out = (own_cols.astype(jnp.float32) + head_share).astype(jnp.bfloat16)
        is_last = row_map[:, None] == (doc_ends - 1)[None, :]
        label_f = doc_labels.astype(jnp.float32)
        harmful = jnp.sum(label_f)
        harmless = doc_labels.shape[0] - jnp.sum(label_f)
        stream = residual_out.astype(jnp.float32)
        harm_rows = jnp.sum(jnp.where(is_last, label_f[None, :], 0.0), 1)
        safe_rows = jnp.sum(jnp.where(is_last, (1.0 - label_f)[None, :], 0.0), 1)
        sums = jnp.stack(
            [jnp.sum(harm_rows[:, None] * stream, 0), jnp.sum(safe_rows[:, None] * stream, 0)]
        )
        for axis in (("xh", "c"), "z"):
            sums = lax.psum(sums, axis)
        refusal_direction = sums[0] / harmful - sums[1] / harmless
        return (residual_out, refusal_direction)

    return local


def solution(mesh):
    n_ctx = mesh.shape["ctx"]
    n_head = mesh.shape["head"]
    nc, nxh = (2, 2)
    nz = n_ctx // (nc * nxh)
    ny, nxl = (n_head // 2, 2)
    fine = Mesh(mesh.devices.reshape(nz, nxh, nc, ny, nxl), ("z", "xh", "c", "y", "xl"))
    placed = (
        P(CTX, None),
        P(),
        P(CTX, HEAD),
        P(CTX, HEAD),
        P(CTX, HEAD),
        P(HEAD, CTX),
        P(CTX),
        P(),
        P(),
    )
    return jax.shard_map(
        make_local((nz, nxh, nc), (ny, nxl)),
        mesh=fine,
        in_specs=placed,
        out_specs=(P(CTX, HEAD), P(HEAD)),
        check_vma=False,
    )
```

profile of v0, /device:TPU:8, one launch (start us, length us, event | category | flops | bytes accessed | tf_op | source)
XLA Modules:
  0.0 339.4 jit_solution(16196009366355087545)
XLA Ops:
  14.0 4.9 %collective-permute-start.1 = (bf16[128,1024]{0,1:T(8,128)(2,1)S(1)}, bf16[128,1024]{0,1:T(8,128)(2,1)S(1)}, u32[]{:S(2)}, u32[]{:S(2)}) collective-permute-start(bf16[128,1024]{0,1:T(8,128)(2,1)S(1)} %get-tuple-element.60), channel_id=1, source_target_pairs={{0,16},{8,24},{16,0},{24,8},{1,17},{9,25},{17,1},{25,9},{2,18},{10... | collective-permute-start | bytes 786440 | tf_op jit(solution)/shard_map/ppermute | solution.py:132
  21.2 5.3 %collective-permute-done.1 = bf16[128,1024]{0,1:T(8,128)(2,1)S(1)} collective-permute-done((bf16[128,1024]{0,1:T(8,128)(2,1)S(1)}, bf16[128,1024]{0,1:T(8,128)(2,1)S(1)}, u32[]{:S(2)}, u32[]{:S(2)}) %collective-permute-start.1) | collective-permute-done | bytes 262176 | tf_op jit(solution)/shard_map/ppermute | solution.py:132
  26.5 4.9 %collective-permute-done.2 = bf16[128,1024]{0,1:T(8,128)(2,1)} collective-permute-done((bf16[128,1024]{0,1:T(8,128)(2,1)S(1)}, bf16[128,1024]{0,1:T(8,128)(2,1)}, u32[]{:S(2)}, u32[]{:S(2)}) %collective-permute-start.2) | collective-permute-done | bytes 262176 | tf_op jit(solution)/shard_map/ppermute | solution.py:132
  31.4 58.0 %all-gather.3.cloned.1.call-done = bf16[1024,1280]{1,0:T(8,128)(2,1)} async-done(((bf16[64,1280]{1,0:T(8,128)(2,1)}), bf16[1024,1280]{1,0:T(8,128)(2,1)}) %all-gather.3.cloned.1.call-update) | async-done | bytes 2621456 | tf_op jit(solution)/shard_map/all_gather | solution.py:56
  97.5 4.9 %collective-permute-start.4 = (f32[128,768]{0,1:T(8,128)S(1)}, f32[128,768]{0,1:T(8,128)S(1)}, u32[]{:S(2)}, u32[]{:S(2)}) collective-permute-start(f32[128,768]{0,1:T(8,128)S(1)} %slice_add_fusion), channel_id=1, source_target_pairs={{0,16},{8,24},{16,0},{24,8},{1,17},{9,25},{17,1},{25,9},{2,18},{10... | collective-permute-start | bytes 1179656 | tf_op jit(solution)/shard_map/ppermute | solution.py:141
  102.6 9.5 %collective-permute-done.4 = f32[128,768]{0,1:T(8,128)S(1)} collective-permute-done((f32[128,768]{0,1:T(8,128)S(1)}, f32[128,768]{0,1:T(8,128)S(1)}, u32[]{:S(2)}, u32[]{:S(2)}) %collective-permute-start.4) | collective-permute-done | bytes 393248 | tf_op jit(solution)/shard_map/ppermute | solution.py:141
  116.8 4.9 %collective-permute-start.7 = (bf16[1024,512]{1,0:T(8,128)(2,1)S(1)}, bf16[1024,512]{1,0:T(8,128)(2,1)}, u32[]{:S(2)}, u32[]{:S(2)}) collective-permute-start(bf16[1024,512]{1,0:T(8,128)(2,1)S(1)} %slice.159), channel_id=1, source_target_pairs={{0,16},{16,0},{1,17},{17,1},{2,18},{18,2},{3,19},{19,3},{4,20},{20... | collective-permute-start | bytes 3145736 | tf_op jit(solution)/shard_map/ppermute | solution.py:52
  121.7 62.2 %all-gather.5.cloned.1.call-done = bf16[2176,256]{1,0:T(8,128)(2,1)} async-done(((bf16[136,256]{1,0:T(8,128)(2,1)}), bf16[2176,256]{1,0:T(8,128)(2,1)}) %all-gather.5.cloned.1.call-update) | async-done | bytes 1114128 | tf_op jit(solution)/shard_map/all_gather | solution.py:56
  183.9 4.9 %collective-permute-start.5 = (bf16[2176,256]{1,0:T(8,128)(2,1)}, bf16[2176,256]{1,0:T(8,128)(2,1)S(1)}, u32[]{:S(2)}, u32[]{:S(2)}) collective-permute-start(bf16[2176,256]{1,0:T(8,128)(2,1)} %all-gather.5.cloned.1.call-done), channel_id=1, source_target_pairs={{0,16},{16,0},{1,17},{17,1},{2,18},{18,2},{3,19},{19,3},{4,20},{20... | collective-permute-start | bytes 3342344 | tf_op jit(solution)/shard_map/ppermute | solution.py:52
  188.8 2.7 pad_maximum_fusion.3
  193.6 11.2 %collective-permute-done.5 = bf16[2176,256]{1,0:T(8,128)(2,1)S(1)} collective-permute-done((bf16[2176,256]{1,0:T(8,128)(2,1)}, bf16[2176,256]{1,0:T(8,128)(2,1)S(1)}, u32[]{:S(2)}, u32[]{:S(2)}) %collective-permute-start.5) | collective-permute-done | bytes 1114144 | tf_op jit(solution)/shard_map/ppermute | solution.py:52
  214.3 3.6 %pad_maximum_fusion.1 = bf16[4096,512]{1,0:T(8,128)(2,1)} fusion(bf16[2048,512]{1,0:T(8,128)(2,1)} %collective-permute-done.8, bf16[1024,512]{1,0:T(8,128)(2,1)} %collective-permute-done.7, bf16[1024,512]{1,0:T(8,128)(2,1)S(1)} %slice.159), kind=kLoop, calls=%fused_computation.14 | loop fusion | flops 12582912 | bytes 8388608 | tf_op jit(solution)/shard_map/concatenate | solution.py:52
  217.9 11.3 %pad_maximum_fusion = bf16[8704,256]{1,0:T(8,128)(2,1)S(1)} fusion(bf16[4352,256]{1,0:T(8,128)(2,1)} %collective-permute-done.6, bf16[2176,256]{1,0:T(8,128)(2,1)S(1)} %copy-done.2, bf16[2176,256]{1,0:T(8,128)(2,1)S(1)} %copy-done), kind=kLoop, calls=%fused_computation.13 | loop fusion | flops 13369344 | bytes 8912896 | tf_op jit(solution)/shard_map/concatenate | solution.py:52
  235.2 2.9 gather_fusion.2
  238.5 4.5 %fusion.63 = (f32[2,4,64]{2,1,0:T(4,128)S(1)}, bf16[2,4,64,2112]{3,2,1,0:T(8,128)(2,1)}) fusion(pred[2,64,2112]{2,1,0:T(8,128)(4,1)S(1)} %compare_and_fusion, bf16[2,2112,256]{2,1,0:T(8,128)(2,1)S(1)} %bitcast.117, bf16[2,64,4,64]{3,1,2,0:T(8,128)(2,1)} %copy.98, bf16[2,64,4,64]{3,1,2,0:T(8,128)(2,1)} %copy.97), kind=kOutput, calls=%fused_computation.145 | convolution fusion | flops 283576384 | bytes 3934208 | tf_op jit(solution)/shard_map/sub | solution.py:187
  245.6 3.4 %fusion.40 = f32[128,2,2,16,64]{0,4,3,2,1:T(8,128)S(1)} fusion(bf16[2,2,16,64,512]{4,3,2,1,0:T(8,128)(2,1)} %bitcast.111, bf16[128,512,1,1,1]{1,0,2,3,4:T(8,128)(2,1)S(1)} %reshape.594), kind=kOutput, calls=%fused_computation.71 | convolution fusion | flops 536870912 | bytes 6422528 | tf_op jit(solution)/shard_map/tk,jdk->tjd/dot_general | solution.py:199
  251.0 3.3 select_bitcast_fusion.1
  258.1 2.8 collective-permute-start.9
  261.0 13.6 %collective-permute-done.9 = bf16[128,4,512]{0,2,1:T(8,128)(2,1)} collective-permute-done((bf16[128,4,512]{0,2,1:T(8,128)(2,1)}, bf16[128,4,512]{0,2,1:T(8,128)(2,1)}, u32[]{:S(2)}, u32[]{:S(2)}) %collective-permute-start.9) | collective-permute-done | bytes 524320 | tf_op jit(solution)/shard_map/ppermute | solution.py:94
  276.9 3.4 collective-permute-start.10
  280.3 3.1 collective-permute-start.11
  283.3 4.0 %collective-permute-start.12 = (bf16[128,512]{0,1:T(8,128)(2,1)S(1)}, bf16[128,512]{0,1:T(8,128)(2,1)S(1)}, u32[]{:S(2)}, u32[]{:S(2)}) collective-permute-start(bf16[128,512]{0,1:T(8,128)(2,1)S(1)} %get-tuple-element.56), channel_id=1, source_target_pairs={{0,6},{2,0},{4,2},{6,4},{1,7},{3,1},{5,3},{7,5},{8,14},{10,8},{12,... | collective-permute-start | bytes 393224 | tf_op jit(solution)/shard_map/ppermute | solution.py:98
  292.5 8.5 %psum.14 = f32[2,512]{1,0:T(2,128)S(1)} all-reduce(f32[2,512]{1,0:T(2,128)S(1)} %pad_maximum_fusion.12), channel_id=1, replica_groups=mesh['z'=16,'xh'=2,'c'=2,'y'=4,'xl'=2] {'xh','c'}, use_global_device_ids=true, to_apply=%region_11.15 | all-reduce | flops 1024 | bytes 8192 | tf_op jit(solution)/shard_map/psum | solution.py:217
  301.0 29.5 %psum.15 = f32[2,512]{1,0:T(2,128)S(1)} all-reduce(f32[2,512]{1,0:T(2,128)S(1)} %psum.14), channel_id=1, replica_groups=mesh['z'=16,'xh'=2,'c'=2,'y'=4,'xl'=2] {'z'}, use_global_device_ids=true, to_apply=%region_12.16 | all-reduce | flops 1024 | bytes 8192 | tf_op jit(solution)/shard_map/psum | solution.py:217
  (123 shorter events, 56.6 us)
Async XLA Ops:
  7.2 4.0 %copy-start.5 = (f32[4096]{0:T(1024)S(1)}, f32[4096]{0:T(1024)}, u32[]{:S(2)}) copy-start(f32[4096]{0:T(1024)} %param.16) | copy-start | bytes 49156
  7.2 82.3 %all-gather.3.cloned.1.call-start = ((), (), s32[]{:S(2)}) async-start(), calls=%async_computation | async-start | bytes 2785280 | tf_op jit(solution)/shard_map/all_gather | solution.py:56
  8.8 175.0 %all-gather.5.cloned.1.call-start = ((), (), s32[]{:S(2)}) async-start(), calls=%async_computation.1 | async-start | bytes 1183744 | tf_op jit(solution)/shard_map/all_gather | solution.py:56
  12.1 9.1 %collective-permute-start = (bf16[128,1024]{0,1:T(8,128)(2,1)S(1)}, bf16[128,1024]{0,1:T(8,128)(2,1)S(1)}, u32[]{:S(2)}, u32[]{:S(2)}) collective-permute-start(bf16[128,1024]{0,1:T(8,128)(2,1)S(1)} %get-tuple-element.61), channel_id=1, source_target_pairs={{0,8},{8,0},{16,24},{24,16},{1,9},{9,1},{17,25},{25,17},{2,10},{10... | collective-permute-start | bytes 786440 | tf_op jit(solution)/shard_map/ppermute | solution.py:132
  14.0 12.5 %collective-permute-start.1 = (bf16[128,1024]{0,1:T(8,128)(2,1)S(1)}, bf16[128,1024]{0,1:T(8,128)(2,1)S(1)}, u32[]{:S(2)}, u32[]{:S(2)}) collective-permute-start(bf16[128,1024]{0,1:T(8,128)(2,1)S(1)} %get-tuple-element.60), channel_id=1, source_target_pairs={{0,16},{8,24},{16,0},{24,8},{1,17},{9,25},{17,1},{25,9},{2,18},{10... | collective-permute-start | bytes 786440 | tf_op jit(solution)/shard_map/ppermute | solution.py:132
  18.9 12.5 %collective-permute-start.2 = (bf16[128,1024]{0,1:T(8,128)(2,1)S(1)}, bf16[128,1024]{0,1:T(8,128)(2,1)}, u32[]{:S(2)}, u32[]{:S(2)}) collective-permute-start(bf16[128,1024]{0,1:T(8,128)(2,1)S(1)} %get-tuple-element.59), channel_id=1, source_target_pairs={{0,24},{8,16},{16,8},{24,0},{1,25},{9,17},{17,9},{25,1},{2,26},{10... | collective-permute-start | bytes 786440 | tf_op jit(solution)/shard_map/ppermute | solution.py:132
  92.0 2.3 copy-start.9
  92.1 4.3 %collective-permute-start.3 = (f32[256,768]{0,1:T(8,128)S(1)}, f32[256,768]{0,1:T(8,128)}, u32[]{:S(2)}, u32[]{:S(2)}) collective-permute-start(f32[256,768]{0,1:T(8,128)S(1)} %pad_maximum_fusion.4), channel_id=1, source_target_pairs={{0,8},{8,0},{16,24},{24,16},{1,9},{9,1},{17,25},{25,17},{2,10},{10... | collective-permute-start | bytes 2359304 | tf_op jit(solution)/shard_map/ppermute | solution.py:138
  97.5 14.6 %collective-permute-start.4 = (f32[128,768]{0,1:T(8,128)S(1)}, f32[128,768]{0,1:T(8,128)S(1)}, u32[]{:S(2)}, u32[]{:S(2)}) collective-permute-start(f32[128,768]{0,1:T(8,128)S(1)} %slice_add_fusion), channel_id=1, source_target_pairs={{0,16},{8,24},{16,0},{24,8},{1,17},{9,25},{17,1},{25,9},{2,18},{10... | collective-permute-start | bytes 1179656 | tf_op jit(solution)/shard_map/ppermute | solution.py:141
  116.8 72.0 %collective-permute-start.7 = (bf16[1024,512]{1,0:T(8,128)(2,1)S(1)}, bf16[1024,512]{1,0:T(8,128)(2,1)}, u32[]{:S(2)}, u32[]{:S(2)}) collective-permute-start(bf16[1024,512]{1,0:T(8,128)(2,1)S(1)} %slice.159), channel_id=1, source_target_pairs={{0,16},{16,0},{1,17},{17,1},{2,18},{18,2},{3,19},{19,3},{4,20},{20... | collective-permute-start | bytes 3145736 | tf_op jit(solution)/shard_map/ppermute | solution.py:52
  183.9 20.9 %copy-start = (bf16[2176,256]{1,0:T(8,128)(2,1)S(1)}, bf16[2176,256]{1,0:T(8,128)(2,1)}, u32[]{:S(2)}) copy-start(bf16[2176,256]{1,0:T(8,128)(2,1)} %all-gather.5.cloned.1.call-done) | copy-start | bytes 3342340
  183.9 20.8 %collective-permute-start.5 = (bf16[2176,256]{1,0:T(8,128)(2,1)}, bf16[2176,256]{1,0:T(8,128)(2,1)S(1)}, u32[]{:S(2)}, u32[]{:S(2)}) collective-permute-start(bf16[2176,256]{1,0:T(8,128)(2,1)} %all-gather.5.cloned.1.call-done), channel_id=1, source_target_pairs={{0,16},{16,0},{1,17},{17,1},{2,18},{18,2},{3,19},{19,3},{4,20},{20... | collective-permute-start | bytes 3342344 | tf_op jit(solution)/shard_map/ppermute | solution.py:52
  191.5 18.7 %slice-start = ((f32[128,768]{0,1:T(8,128)}), f32[128,512]{0,1:T(8,128)S(1)}, s32[]{:S(2)}) async-start(f32[128,768]{0,1:T(8,128)} %copy-done.4), calls=%async_computation.2 | async-start | bytes 524288 | tf_op jit(solution)/shard_map/slice | solution.py:143
  191.5 22.8 %collective-permute-start.8 = (bf16[2048,512]{1,0:T(8,128)(2,1)}, bf16[2048,512]{1,0:T(8,128)(2,1)}, u32[]{:S(2)}, u32[]{:S(2)}) collective-permute-start(bf16[2048,512]{1,0:T(8,128)(2,1)} %pad_maximum_fusion.3), channel_id=1, source_target_pairs={{0,8},{8,0},{1,9},{9,1},{2,10},{10,2},{3,11},{11,3},{4,12},{12,4},... | collective-permute-start | bytes 6291464 | tf_op jit(solution)/shard_map/ppermute | solution.py:52
  206.5 11.4 %collective-permute-start.6 = (bf16[4352,256]{1,0:T(8,128)(2,1)}, bf16[4352,256]{1,0:T(8,128)(2,1)}, u32[]{:S(2)}, u32[]{:S(2)}) collective-permute-start(bf16[4352,256]{1,0:T(8,128)(2,1)} %pad_maximum_fusion.2), channel_id=1, source_target_pairs={{0,8},{8,0},{1,9},{9,1},{2,10},{10,2},{3,11},{11,3},{4,12},{12,4},... | collective-permute-start | bytes 6684680 | tf_op jit(solution)/shard_map/ppermute | solution.py:52
  214.3 3.6 %copy-start.2 = (bf16[2176,256]{1,0:T(8,128)(2,1)S(1)}, bf16[2176,256]{1,0:T(8,128)(2,1)}, u32[]{:S(2)}) copy-start(bf16[2176,256]{1,0:T(8,128)(2,1)} %copy-done.1) | copy-start | bytes 3342340
  235.2 3.0 copy-start.12
  257.2 30.1 %copy-start.13 = (s32[32]{0:T(128)S(1)}, s32[32]{0:T(128)}, u32[]{:S(2)}) copy-start(s32[32]{0:T(128)} %param.23) | copy-start | bytes 388
  257.2 31.5 %copy-start.10 = (s32[128]{0:T(128)S(1)}, s32[128]{0:T(128)}, u32[]{:S(2)}) copy-start(s32[128]{0:T(128)} %param.21) | copy-start | bytes 1540
  257.2 31.5 %copy-start.11 = (s32[32]{0:T(128)S(1)}, s32[32]{0:T(128)}, u32[]{:S(2)}) copy-start(s32[32]{0:T(128)} %get-tuple-element.76) | copy-start | bytes 388
  258.1 16.5 %collective-permute-start.9 = (bf16[128,4,512]{0,2,1:T(8,128)(2,1)}, bf16[128,4,512]{0,2,1:T(8,128)(2,1)}, u32[]{:S(2)}, u32[]{:S(2)}) collective-permute-start(bf16[128,4,512]{0,2,1:T(8,128)(2,1)} %bitcast_convert_fusion), channel_id=1, source_target_pairs={{0,1},{1,0},{2,3},{3,2},{4,5},{5,4},{6,7},{7,6},{8,9},{9,8},{10,11... | collective-permute-start | bytes 1572872 | tf_op jit(solution)/shard_map/ppermute | solution.py:94
  276.9 12.0 %collective-permute-start.10 = (bf16[128,512]{0,1:T(8,128)(2,1)S(1)}, bf16[128,512]{0,1:T(8,128)(2,1)S(1)}, u32[]{:S(2)}, u32[]{:S(2)}) collective-permute-start(bf16[128,512]{0,1:T(8,128)(2,1)S(1)} %get-tuple-element.55), channel_id=1, source_target_pairs={{0,2},{2,4},{4,6},{6,0},{1,3},{3,5},{5,7},{7,1},{8,10},{10,12},{12... | collective-permute-start | bytes 393224 | tf_op jit(solution)/shard_map/ppermute | solution.py:98
  280.3 9.5 %collective-permute-start.11 = (bf16[128,512]{0,1:T(8,128)(2,1)S(1)}, bf16[128,512]{0,1:T(8,128)(2,1)S(1)}, u32[]{:S(2)}, u32[]{:S(2)}) collective-permute-start(bf16[128,512]{0,1:T(8,128)(2,1)S(1)} %get-tuple-element.57), channel_id=1, source_target_pairs={{0,4},{2,6},{4,0},{6,2},{1,5},{3,7},{5,1},{7,3},{8,12},{10,14},{12... | collective-permute-start | bytes 393224 | tf_op jit(solution)/shard_map/ppermute | solution.py:98
  283.3 8.0 %collective-permute-start.12 = (bf16[128,512]{0,1:T(8,128)(2,1)S(1)}, bf16[128,512]{0,1:T(8,128)(2,1)S(1)}, u32[]{:S(2)}, u32[]{:S(2)}) collective-permute-start(bf16[128,512]{0,1:T(8,128)(2,1)S(1)} %get-tuple-element.56), channel_id=1, source_target_pairs={{0,6},{2,0},{4,2},{6,4},{1,7},{3,1},{5,3},{7,5},{8,14},{10,8},{12,... | collective-permute-start | bytes 393224 | tf_op jit(solution)/shard_map/ppermute | solution.py:98
  (6 other events, 9.9 us)
Sparse Core Ops, SparseCore 0:
  10.1 79.3 all-gather.2
  115.6 68.1 all-gather.4
where the time goes:
time: 341 us; the launch traced here: 339 us
  waiting for transfers between devices  169 us (50%)
  starting transfers between devices  43 us (13%)
  other arithmetic  38.1 us (11%)
  blocking collectives  38 us (11%)
  local copies, waits for them, and re-layouts  23.5 us (7%)
  between operations  15.4 us (5%)
  matrix products  12.8 us (4%)
    all_gather x2, waiting for transfers between devices, gather_z(): return lax.all_gather(x, 'z', axis=0, tiled=True)  120 us
    psum x2, blocking collectives, local(): sums = lax.psum(sums, axis)  38 us
    concatenate x4, other arithmetic, swap_cat(): return jnp.concatenate([x, lax.ppermute(x, axis_name, [(0, 1), (1, 0)])], 0)  19.3 us
    ppermute x4, starting transfers between devices, swap_cat(): return jnp.concatenate([x, lax.ppermute(x, axis_name, [(0, 1), (1, 0)])], 0)  13.8 us
    ppermute x1, waiting for transfers between devices, reduce_scatter_head(): lax.ppermute(sent, 'xl', [(0, 1), (1, 0)]).astype(jnp.float32)  13.6 us
    ppermute x4, waiting for transfers between devices, swap_cat(): return jnp.concatenate([x, lax.ppermute(x, axis_name, [(0, 1), (1, 0)])], 0)  11.2 us
    ppermute x3, starting transfers between devices, reduce_scatter_head(): lax.ppermute(piece, 'y', [(i, (i + shift) % ny) for i in range(ny)])  10.4 us
    ppermute x3, waiting for transfers between devices, local(): lax.ppermute(jnp.take(quarters, me ^ flip, axis=1), pair, perm)  10.2 us
  transfers between devices with their start and end apart: 15, of which 10 were waited for; matrix products, arithmetic and copies ran while one was open for 6% of the time, Pallas kernels for 0%

commit v1 on v0

--- a/solution.py
+++ b/solution.py
@@ -53,7 +53,7 @@
 
 
 def gather_z(x):
-    return lax.all_gather(x, "z", axis=0, tiled=True)
+    return jnp.concatenate(lax.all_to_all(jnp.stack([x] * lax.axis_size("z")), "z", 0, 0), axis=0)
 
 
 def gather_pair(x):

time: 341 us -> 381 us (1.12)
  waiting for transfers between devices: 169 us -> 193 us
  starting transfers between devices: 43 us -> 66.9 us
  between operations: 15.4 us -> 2.04 us
  blocking collectives: 38 us -> 42.4 us
    all_to_all x0 -> x2, waiting for transfers between devices: none -> 142 us  [gather_z(): lax.all_to_all(jnp.stack([x] * lax.axis_size('z')), 'z', 0, 0)]
    all_gather x2 -> x0, waiting for transfers between devices: 120 us -> none  [gather_z(): return lax.all_gather(x, 'z', axis=0, tiled=True)]
    all_to_all x0 -> x2, starting transfers between devices: none -> 22.9 us  [gather_z(): lax.all_to_all(jnp.stack([x] * lax.axis_size('z')), 'z', 0, 0)]
    psum x2, blocking collectives: 38 us -> 42.4 us  [local(): sums = lax.psum(sums, axis)]
  transfers between devices with their start and end apart: 15 -> 15, of which waited for: 10 -> 10; matrix products, arithmetic and copies ran while one was open for 6% -> 5% of each run, Pallas kernels for 0% -> 0%
where the time goes in v1:
time: 381 us; the launch traced here: 379 us
  waiting for transfers between devices  193 us (51%)
  starting transfers between devices  66.9 us (18%)
  blocking collectives  42.4 us (11%)
  other arithmetic  37.4 us (10%)
  local copies, waits for them, and re-layouts  24.8 us (7%)
  matrix products  12.8 us (3%)
    all_to_all x2, waiting for transfers between devices, gather_z(): lax.all_to_all(jnp.stack([x] * lax.axis_size('z')), 'z', 0, 0)  142 us
    psum x2, blocking collectives, local(): sums = lax.psum(sums, axis)  42.4 us
    all_to_all x2, starting transfers between devices, gather_z(): lax.all_to_all(jnp.stack([x] * lax.axis_size('z')), 'z', 0, 0)  22.9 us
    concatenate x4, other arithmetic, swap_cat(): return jnp.concatenate([x, lax.ppermute(x, axis_name, [(0, 1), (1, 0)])], 0)  19.3 us
    ppermute x4, waiting for transfers between devices, swap_cat(): return jnp.concatenate([x, lax.ppermute(x, axis_name, [(0, 1), (1, 0)])], 0)  14.5 us
    ppermute x4, starting transfers between devices, swap_cat(): return jnp.concatenate([x, lax.ppermute(x, axis_name, [(0, 1), (1, 0)])], 0)  14 us
    ppermute x1, waiting for transfers between devices, reduce_scatter_head(): lax.ppermute(sent, 'xl', [(0, 1), (1, 0)]).astype(jnp.float32)  13.1 us
    ppermute x3, starting transfers between devices, reduce_scatter_head(): lax.ppermute(piece, 'y', [(i, (i + shift) % ny) for i in range(ny)])  10.7 us
  transfers between devices with their start and end apart: 15, of which 10 were waited for; matrix products, arithmetic and copies ran while one was open for 5% of the time, Pallas kernels for 0%

profile of v1, /device:TPU:8, one launch (start us, length us, event | category | flops | bytes accessed | tf_op | source)
XLA Modules:
  0.0 379.2 jit_solution(14696119706966743005)
XLA Ops:
  3.3 15.4 %all-to-all-start = ((bf16[16,64,1280]{2,1,0:T(8,128)(2,1)}), bf16[16,64,1280]{2,1,0:T(8,128)(2,1)}, u32[]{:S(2)}, u32[]{:S(2)}) async-start(bf16[16,64,1280]{2,1,0:T(8,128)(2,1)} %stack.10), calls=%async_computation | async-start | bytes 5242880 | tf_op jit(solution)/shard_map/all_to_all | solution.py:56
  22.9 4.9 %collective-permute-start.1 = (bf16[128,1024]{0,1:T(8,128)(2,1)S(1)}, bf16[128,1024]{0,1:T(8,128)(2,1)S(1)}, u32[]{:S(2)}, u32[]{:S(2)}) collective-permute-start(bf16[128,1024]{0,1:T(8,128)(2,1)S(1)} %get-tuple-element.58), channel_id=1, source_target_pairs={{0,16},{8,24},{16,0},{24,8},{1,17},{9,25},{17,1},{25,9},{2,18},{10... | collective-permute-start | bytes 786440 | tf_op jit(solution)/shard_map/ppermute | solution.py:132
  30.1 5.3 %collective-permute-done.1 = bf16[128,1024]{0,1:T(8,128)(2,1)S(1)} collective-permute-done((bf16[128,1024]{0,1:T(8,128)(2,1)S(1)}, bf16[128,1024]{0,1:T(8,128)(2,1)S(1)}, u32[]{:S(2)}, u32[]{:S(2)}) %collective-permute-start.1) | collective-permute-done | bytes 262176 | tf_op jit(solution)/shard_map/ppermute | solution.py:132
  35.4 4.9 %collective-permute-done.2 = bf16[128,1024]{0,1:T(8,128)(2,1)} collective-permute-done((bf16[128,1024]{0,1:T(8,128)(2,1)S(1)}, bf16[128,1024]{0,1:T(8,128)(2,1)}, u32[]{:S(2)}, u32[]{:S(2)}) %collective-permute-start.2) | collective-permute-done | bytes 262176 | tf_op jit(solution)/shard_map/ppermute | solution.py:132
  40.3 96.2 %all-to-all-done = bf16[16,64,1280]{2,1,0:T(8,128)(2,1)} async-done(((bf16[16,64,1280]{2,1,0:T(8,128)(2,1)}), bf16[16,64,1280]{2,1,0:T(8,128)(2,1)}, u32[]{:S(2)}, u32[]{:S(2)}) %all-to-all-start) | async-done | bytes 2621472 | tf_op jit(solution)/shard_map/all_to_all | solution.py:56
  144.6 4.9 %collective-permute-start.4 = (f32[128,768]{0,1:T(8,128)S(1)}, f32[128,768]{0,1:T(8,128)S(1)}, u32[]{:S(2)}, u32[]{:S(2)}) collective-permute-start(f32[128,768]{0,1:T(8,128)S(1)} %slice_add_fusion), channel_id=1, source_target_pairs={{0,16},{8,24},{16,0},{24,8},{1,17},{9,25},{17,1},{25,9},{2,18},{10... | collective-permute-start | bytes 1179656 | tf_op jit(solution)/shard_map/ppermute | solution.py:141
  149.7 9.4 %collective-permute-done.4 = f32[128,768]{0,1:T(8,128)S(1)} collective-permute-done((f32[128,768]{0,1:T(8,128)S(1)}, f32[128,768]{0,1:T(8,128)S(1)}, u32[]{:S(2)}, u32[]{:S(2)}) %collective-permute-start.4) | collective-permute-done | bytes 393248 | tf_op jit(solution)/shard_map/ppermute | solution.py:141
  163.0 7.5 %all-to-all-start.1 = ((bf16[16,136,256]{2,1,0:T(8,128)(2,1)}), bf16[16,136,256]{2,1,0:T(8,128)(2,1)S(1)}, u32[]{:S(2)}, u32[]{:S(2)}) async-start(bf16[16,136,256]{2,1,0:T(8,128)(2,1)} %stack.11), calls=%async_computation.1 | async-start | bytes 2228224 | tf_op jit(solution)/shard_map/all_to_all | solution.py:56
  171.9 4.9 %collective-permute-start.7 = (bf16[1024,512]{1,0:T(8,128)(2,1)S(1)}, bf16[1024,512]{1,0:T(8,128)(2,1)}, u32[]{:S(2)}, u32[]{:S(2)}) collective-permute-start(bf16[1024,512]{1,0:T(8,128)(2,1)S(1)} %slice.159), channel_id=1, source_target_pairs={{0,16},{16,0},{1,17},{17,1},{2,18},{18,2},{3,19},{19,3},{4,20},{20... | collective-permute-start | bytes 3145736 | tf_op jit(solution)/shard_map/ppermute | solution.py:52
  176.8 45.6 %all-to-all-done.1 = bf16[16,136,256]{2,1,0:T(8,128)(2,1)S(1)} async-done(((bf16[16,136,256]{2,1,0:T(8,128)(2,1)}), bf16[16,136,256]{2,1,0:T(8,128)(2,1)S(1)}, u32[]{:S(2)}, u32[]{:S(2)}) %all-to-all-start.1) | async-done | bytes 1114144 | tf_op jit(solution)/shard_map/all_to_all | solution.py:56
  222.4 4.9 %collective-permute-start.5 = (bf16[2176,256]{1,0:T(8,128)(2,1)S(1)}, bf16[2176,256]{1,0:T(8,128)(2,1)S(1)}, u32[]{:S(2)}, u32[]{:S(2)}) collective-permute-start(bf16[2176,256]{1,0:T(8,128)(2,1)S(1)} %bitcast.114), channel_id=1, source_target_pairs={{0,16},{16,0},{1,17},{17,1},{2,18},{18,2},{3,19},{19,3},{4,20},{20... | collective-permute-start | bytes 3342344 | tf_op jit(solution)/shard_map/ppermute | solution.py:52
  232.1 14.5 %collective-permute-done.5 = bf16[2176,256]{1,0:T(8,128)(2,1)S(1)} collective-permute-done((bf16[2176,256]{1,0:T(8,128)(2,1)S(1)}, bf16[2176,256]{1,0:T(8,128)(2,1)S(1)}, u32[]{:S(2)}, u32[]{:S(2)}) %collective-permute-start.5) | collective-permute-done | bytes 1114144 | tf_op jit(solution)/shard_map/ppermute | solution.py:52
  256.3 3.6 pad_maximum_fusion.1
  259.9 11.3 %pad_maximum_fusion = bf16[8704,256]{1,0:T(8,128)(2,1)S(1)} fusion(bf16[4352,256]{1,0:T(8,128)(2,1)} %collective-permute-done.6, bf16[2176,256]{1,0:T(8,128)(2,1)S(1)} %copy-done.1, bf16[2176,256]{1,0:T(8,128)(2,1)S(1)} %bitcast.116), kind=kLoop, calls=%fused_computation.13 | loop fusion | flops 13369344 | bytes 8912896 | tf_op jit(solution)/shard_map/concatenate | solution.py:52
  277.3 2.9 gather_fusion.2
  280.6 4.5 %fusion.63 = (f32[2,4,64]{2,1,0:T(4,128)S(1)}, bf16[2,4,64,2112]{3,2,1,0:T(8,128)(2,1)}) fusion(pred[2,64,2112]{2,1,0:T(8,128)(4,1)S(1)} %compare_and_fusion, bf16[2,2112,256]{2,1,0:T(8,128)(2,1)S(1)} %bitcast.122, bf16[2,64,4,64]{3,1,2,0:T(8,128)(2,1)} %copy.77, bf16[2,64,4,64]{3,1,2,0:T(8,128)(2,1)} %copy.76), kind=kOutput, calls=%fused_computation.145 | convolution fusion | flops 283576384 | bytes 3934208 | tf_op jit(solution)/shard_map/sub | solution.py:187
  287.7 3.4 fusion.40
  293.1 3.3 select_bitcast_fusion.1
  300.2 3.4 collective-permute-start.9
  303.7 13.1 %collective-permute-done.9 = bf16[128,4,512]{0,2,1:T(8,128)(2,1)} collective-permute-done((bf16[128,4,512]{0,2,1:T(8,128)(2,1)}, bf16[128,4,512]{0,2,1:T(8,128)(2,1)}, u32[]{:S(2)}, u32[]{:S(2)}) %collective-permute-start.9) | collective-permute-done | bytes 524320 | tf_op jit(solution)/shard_map/ppermute | solution.py:94
  319.0 3.5 collective-permute-start.10
  325.3 4.3 %collective-permute-start.12 = (bf16[128,512]{0,1:T(8,128)(2,1)S(1)}, bf16[128,512]{0,1:T(8,128)(2,1)S(1)}, u32[]{:S(2)}, u32[]{:S(2)}) collective-permute-start(bf16[128,512]{0,1:T(8,128)(2,1)S(1)} %get-tuple-element.54), channel_id=1, source_target_pairs={{0,6},{2,0},{4,2},{6,4},{1,7},{3,1},{5,3},{7,5},{8,14},{10,8},{12,... | collective-permute-start | bytes 393224 | tf_op jit(solution)/shard_map/ppermute | solution.py:98
  334.7 9.2 %psum.14 = f32[2,512]{1,0:T(2,128)S(1)} all-reduce(f32[2,512]{1,0:T(2,128)S(1)} %pad_maximum_fusion.12), channel_id=1, replica_groups=mesh['z'=16,'xh'=2,'c'=2,'y'=4,'xl'=2] {'xh','c'}, use_global_device_ids=true, to_apply=%region_11.15 | all-reduce | flops 1024 | bytes 8192 | tf_op jit(solution)/shard_map/psum | solution.py:217
  343.9 33.3 %psum.15 = f32[2,512]{1,0:T(2,128)S(1)} all-reduce(f32[2,512]{1,0:T(2,128)S(1)} %psum.14), channel_id=1, replica_groups=mesh['z'=16,'xh'=2,'c'=2,'y'=4,'xl'=2] {'z'}, use_global_device_ids=true, to_apply=%region_12.16 | all-reduce | flops 1024 | bytes 8192 | tf_op jit(solution)/shard_map/psum | solution.py:217
  (123 shorter events, 62.8 us)
Async XLA Ops:
  3.3 15.4 %copy-start.4 = (bf16[128,4096]{1,0:T(8,128)(2,1)S(1)}, bf16[128,4096]{1,0:T(8,128)(2,1)}, u32[]{:S(2)}) copy-start(bf16[128,4096]{1,0:T(8,128)(2,1)} %param.15) | copy-start | bytes 3145732
  3.3 133.2 %all-to-all-start = ((bf16[16,64,1280]{2,1,0:T(8,128)(2,1)}), bf16[16,64,1280]{2,1,0:T(8,128)(2,1)}, u32[]{:S(2)}, u32[]{:S(2)}) async-start(bf16[16,64,1280]{2,1,0:T(8,128)(2,1)} %stack.10), calls=%async_computation | async-start | bytes 5242880 | tf_op jit(solution)/shard_map/all_to_all | solution.py:56
  21.0 9.1 %collective-permute-start = (bf16[128,1024]{0,1:T(8,128)(2,1)S(1)}, bf16[128,1024]{0,1:T(8,128)(2,1)S(1)}, u32[]{:S(2)}, u32[]{:S(2)}) collective-permute-start(bf16[128,1024]{0,1:T(8,128)(2,1)S(1)} %get-tuple-element.59), channel_id=1, source_target_pairs={{0,8},{8,0},{16,24},{24,16},{1,9},{9,1},{17,25},{25,17},{2,10},{10... | collective-permute-start | bytes 786440 | tf_op jit(solution)/shard_map/ppermute | solution.py:132
  22.9 12.5 %collective-permute-start.1 = (bf16[128,1024]{0,1:T(8,128)(2,1)S(1)}, bf16[128,1024]{0,1:T(8,128)(2,1)S(1)}, u32[]{:S(2)}, u32[]{:S(2)}) collective-permute-start(bf16[128,1024]{0,1:T(8,128)(2,1)S(1)} %get-tuple-element.58), channel_id=1, source_target_pairs={{0,16},{8,24},{16,0},{24,8},{1,17},{9,25},{17,1},{25,9},{2,18},{10... | collective-permute-start | bytes 786440 | tf_op jit(solution)/shard_map/ppermute | solution.py:132
  27.8 12.5 %collective-permute-start.2 = (bf16[128,1024]{0,1:T(8,128)(2,1)S(1)}, bf16[128,1024]{0,1:T(8,128)(2,1)}, u32[]{:S(2)}, u32[]{:S(2)}) collective-permute-start(bf16[128,1024]{0,1:T(8,128)(2,1)S(1)} %get-tuple-element.57), channel_id=1, source_target_pairs={{0,24},{8,16},{16,8},{24,0},{1,25},{9,17},{17,9},{25,1},{2,26},{10... | collective-permute-start | bytes 786440 | tf_op jit(solution)/shard_map/ppermute | solution.py:132
  139.1 2.3 copy-start.9
  139.2 4.3 %collective-permute-start.3 = (f32[256,768]{0,1:T(8,128)S(1)}, f32[256,768]{0,1:T(8,128)}, u32[]{:S(2)}, u32[]{:S(2)}) collective-permute-start(f32[256,768]{0,1:T(8,128)S(1)} %pad_maximum_fusion.4), channel_id=1, source_target_pairs={{0,8},{8,0},{16,24},{24,16},{1,9},{9,1},{17,25},{25,17},{2,10},{10... | collective-permute-start | bytes 2359304 | tf_op jit(solution)/shard_map/ppermute | solution.py:138
  144.6 14.6 %collective-permute-start.4 = (f32[128,768]{0,1:T(8,128)S(1)}, f32[128,768]{0,1:T(8,128)S(1)}, u32[]{:S(2)}, u32[]{:S(2)}) collective-permute-start(f32[128,768]{0,1:T(8,128)S(1)} %slice_add_fusion), channel_id=1, source_target_pairs={{0,16},{8,24},{16,0},{24,8},{1,17},{9,25},{17,1},{25,9},{2,18},{10... | collective-permute-start | bytes 1179656 | tf_op jit(solution)/shard_map/ppermute | solution.py:141
  163.0 59.3 %all-to-all-start.1 = ((bf16[16,136,256]{2,1,0:T(8,128)(2,1)}), bf16[16,136,256]{2,1,0:T(8,128)(2,1)S(1)}, u32[]{:S(2)}, u32[]{:S(2)}) async-start(bf16[16,136,256]{2,1,0:T(8,128)(2,1)} %stack.11), calls=%async_computation.1 | async-start | bytes 2228224 | tf_op jit(solution)/shard_map/all_to_all | solution.py:56
  171.9 55.5 %collective-permute-start.7 = (bf16[1024,512]{1,0:T(8,128)(2,1)S(1)}, bf16[1024,512]{1,0:T(8,128)(2,1)}, u32[]{:S(2)}, u32[]{:S(2)}) collective-permute-start(bf16[1024,512]{1,0:T(8,128)(2,1)S(1)} %slice.159), channel_id=1, source_target_pairs={{0,16},{16,0},{1,17},{17,1},{2,18},{18,2},{3,19},{19,3},{4,20},{20... | collective-permute-start | bytes 3145736 | tf_op jit(solution)/shard_map/ppermute | solution.py:52
  222.4 24.2 %collective-permute-start.5 = (bf16[2176,256]{1,0:T(8,128)(2,1)S(1)}, bf16[2176,256]{1,0:T(8,128)(2,1)S(1)}, u32[]{:S(2)}, u32[]{:S(2)}) collective-permute-start(bf16[2176,256]{1,0:T(8,128)(2,1)S(1)} %bitcast.114), channel_id=1, source_target_pairs={{0,16},{16,0},{1,17},{17,1},{2,18},{18,2},{3,19},{19,3},{4,20},{20... | collective-permute-start | bytes 3342344 | tf_op jit(solution)/shard_map/ppermute | solution.py:52
  230.0 22.2 %slice-start = ((f32[128,768]{0,1:T(8,128)}), f32[128,512]{0,1:T(8,128)S(1)}, s32[]{:S(2)}) async-start(f32[128,768]{0,1:T(8,128)} %copy-done.3), calls=%async_computation.2 | async-start | bytes 524288 | tf_op jit(solution)/shard_map/slice | solution.py:143
  230.0 26.3 %collective-permute-start.8 = (bf16[2048,512]{1,0:T(8,128)(2,1)}, bf16[2048,512]{1,0:T(8,128)(2,1)}, u32[]{:S(2)}, u32[]{:S(2)}) collective-permute-start(bf16[2048,512]{1,0:T(8,128)(2,1)} %pad_maximum_fusion.3), channel_id=1, source_target_pairs={{0,8},{8,0},{1,9},{9,1},{2,10},{10,2},{3,11},{11,3},{4,12},{12,4},... | collective-permute-start | bytes 6291464 | tf_op jit(solution)/shard_map/ppermute | solution.py:52
  248.4 11.6 %collective-permute-start.6 = (bf16[4352,256]{1,0:T(8,128)(2,1)}, bf16[4352,256]{1,0:T(8,128)(2,1)}, u32[]{:S(2)}, u32[]{:S(2)}) collective-permute-start(bf16[4352,256]{1,0:T(8,128)(2,1)} %pad_maximum_fusion.2), channel_id=1, source_target_pairs={{0,8},{8,0},{1,9},{9,1},{2,10},{10,2},{3,11},{11,3},{4,12},{12,4},... | collective-permute-start | bytes 6684680 | tf_op jit(solution)/shard_map/ppermute | solution.py:52
  256.3 3.6 copy-start.1
  277.3 3.0 copy-start.12
  296.5 2.3 copy-start.6
  299.3 30.4 %copy-start.13 = (s32[32]{0:T(128)S(1)}, s32[32]{0:T(128)}, u32[]{:S(2)}) copy-start(s32[32]{0:T(128)} %param.23) | copy-start | bytes 388
  299.3 31.7 %copy-start.10 = (s32[128]{0:T(128)S(1)}, s32[128]{0:T(128)}, u32[]{:S(2)}) copy-start(s32[128]{0:T(128)} %param.21) | copy-start | bytes 1540
  299.3 31.7 %copy-start.11 = (s32[32]{0:T(128)S(1)}, s32[32]{0:T(128)}, u32[]{:S(2)}) copy-start(s32[32]{0:T(128)} %get-tuple-element.74) | copy-start | bytes 388
  300.2 16.5 %collective-permute-start.9 = (bf16[128,4,512]{0,2,1:T(8,128)(2,1)}, bf16[128,4,512]{0,2,1:T(8,128)(2,1)}, u32[]{:S(2)}, u32[]{:S(2)}) collective-permute-start(bf16[128,4,512]{0,2,1:T(8,128)(2,1)} %bitcast_convert_fusion), channel_id=1, source_target_pairs={{0,1},{1,0},{2,3},{3,2},{4,5},{5,4},{6,7},{7,6},{8,9},{9,8},{10,11... | collective-permute-start | bytes 1572872 | tf_op jit(solution)/shard_map/ppermute | solution.py:94
  319.0 12.2 %collective-permute-start.10 = (bf16[128,512]{0,1:T(8,128)(2,1)S(1)}, bf16[128,512]{0,1:T(8,128)(2,1)S(1)}, u32[]{:S(2)}, u32[]{:S(2)}) collective-permute-start(bf16[128,512]{0,1:T(8,128)(2,1)S(1)} %get-tuple-element.53), channel_id=1, source_target_pairs={{0,2},{2,4},{4,6},{6,0},{1,3},{3,5},{5,7},{7,1},{8,10},{10,12},{12... | collective-permute-start | bytes 393224 | tf_op jit(solution)/shard_map/ppermute | solution.py:98
  322.5 9.5 %collective-permute-start.11 = (bf16[128,512]{0,1:T(8,128)(2,1)S(1)}, bf16[128,512]{0,1:T(8,128)(2,1)S(1)}, u32[]{:S(2)}, u32[]{:S(2)}) collective-permute-start(bf16[128,512]{0,1:T(8,128)(2,1)S(1)} %get-tuple-element.55), channel_id=1, source_target_pairs={{0,4},{2,6},{4,0},{6,2},{1,5},{3,7},{5,1},{7,3},{8,12},{10,14},{12... | collective-permute-start | bytes 393224 | tf_op jit(solution)/shard_map/ppermute | solution.py:98
  325.3 8.2 %collective-permute-start.12 = (bf16[128,512]{0,1:T(8,128)(2,1)S(1)}, bf16[128,512]{0,1:T(8,128)(2,1)S(1)}, u32[]{:S(2)}, u32[]{:S(2)}) collective-permute-start(bf16[128,512]{0,1:T(8,128)(2,1)S(1)} %get-tuple-element.54), channel_id=1, source_target_pairs={{0,6},{2,0},{4,2},{6,4},{1,7},{3,1},{5,3},{7,5},{8,14},{10,8},{12,... | collective-permute-start | bytes 393224 | tf_op jit(solution)/shard_map/ppermute | solution.py:98
  (6 other events, 9.0 us)
